TPU v7x, 32 devices: a whole 2x2x4 slice. The times are simulated.
32 devices in a mesh: groups: 2 (over y), events: 8 (over z, x), heads: 2 (over core).
Axes of the slice: x: 2, y: 2, z: 4, core: 2. Of those that a mesh axis runs over, the one named last changes fastest.
Arguments:
- inputs: bfloat16 [256, 1024], P(('groups', 'events')), parts along dimension 0, may hold values from -6 to 6
- cand_user: int32 [256], P('groups'), parts along dimension 0, may hold values from 0 to 3, as said below
- event_user: int32 [8192], P(('groups', 'events')), parts along dimension 0, may hold values from 0 to 3, as said below
- event_count: int32 [16], P(('groups', 'events')), parts along dimension 0, may hold values from 128 to 512, as said below
- w_qu: bfloat16 [1024, 2, 1024], P(None, None, 'heads'), may hold values from -0.1875 to 0.1875
- keys: bfloat16 [8192, 1024], P(('groups', 'events'), 'heads'), parts along dimension 0, may hold values from -6 to 6
- values: bfloat16 [8192, 1024], P(('groups', 'events'), 'heads'), parts along dimension 0, may hold values from -6 to 6
- gain: float32 [1024], P('heads'), may hold values from 0.1 to 1.9
- w_out: bfloat16 [1024, 1024], P('heads'), may hold values from -0.1875 to 0.1875
Outputs:
- scored: bfloat16 [256, 1024], P(('groups', 'events')), parts along dimension 0
There are 2 independent parts, one for each index of `groups`. A program takes and returns all parts, laid end to end along the dimension named above; an argument that names none is the same for every part. Nothing has to cross between parts.
Inputs may be any that keep to these rules, and one draw needn't show every extreme that they name: `event_count`: each cache shard's filled slots come first; some shard is full and some holds 128. `event_user`: Users' events are consecutive and in increasing user order over the whole cache; every user has 1 to 2047 events, and some user has exactly 2047. `cand_user`: every candidate belongs to a user that has at least one filled slot somewhere in the cache.
All inputs are finite; a program needn't handle non-finite values.
Results may differ from a plain program's by a relative error of at most 0.0075.
Values may be sent and summed in bfloat16 or wider, within the bound.
No kernel may reach another device: no remote copies, remote signals or barrier semaphores. Data moves between devices by JAX's collectives and lax.ppermute only.
A program may use at most 64 MiB of HBM per device.

v0:
```python
import math
import jax
import jax.numpy as jnp
from jax import lax
from jax.sharding import PartitionSpec as P

DH = 128
HD = 1024
epsilon = 1e-05


def shards(inputs, cand_user, event_user, event_count, w_qu, keys, values, gain, w_out):
    row_count = inputs.shape[0]
    feat_width = inputs.shape[1]
    local_width = w_qu.shape[2]
    heads_here = local_width // DH
    slot_total = keys.shape[0]
    score_scale = 1.0 / math.sqrt(DH)
    packed_weight = w_qu.reshape(feat_width, 2 * local_width)
    query_weight = packed_weight[:, :local_width]
    gate_weight = packed_weight[:, local_width:]
    gate_values = jax.nn.silu(
        jnp.dot(inputs, gate_weight, preferred_element_type=jnp.float32)
    ).astype(jnp.bfloat16)
    gathered_rows = lax.all_gather(inputs, "events", axis=0, tiled=True)
    queries = jax.nn.silu(
        jnp.dot(gathered_rows, query_weight, preferred_element_type=jnp.float32)
    ).astype(jnp.bfloat16)
    slot_index = jnp.arange(slot_total, dtype=jnp.int32)
    slot_valid = slot_index < event_count[0]
    key_heads = keys.reshape(slot_total, heads_here, DH)
    value_heads = values.reshape(slot_total, heads_here, DH)

    def attend_rows(query_rows, row_users):
        rows_here = query_rows.shape[0]
        query_block = query_rows.reshape(rows_here, heads_here, DH)
        user_match = ((row_users[:, None] == event_user[None, :]) & slot_valid[None, :]).astype(
            jnp.float32
        )
        scores = (
            jnp.einsum("chd,ehd->hce", query_block, key_heads, preferred_element_type=jnp.float32)
            * score_scale
        )
        attn_weights = (jax.nn.silu(scores) * user_match[None]).astype(jnp.bfloat16)
        partial_out = jnp.einsum(
            "hce,ehd->chd", attn_weights, value_heads, preferred_element_type=jnp.float32
        )
        return partial_out.reshape(rows_here, local_width)

    block_rows = math.gcd(row_count * lax.axis_size("events"), 512)
    block_count = row_count * lax.axis_size("events") // block_rows

    def compute_block(which_block):
        block_start = which_block * block_rows
        query_rows = lax.dynamic_slice_in_dim(queries, block_start, block_rows, 0)
        block_users = lax.dynamic_slice_in_dim(cand_user, block_start, block_rows, 0)
        return attend_rows(query_rows, block_users)

    stacked = lax.map(compute_block, jnp.arange(block_count, dtype=jnp.int32))
    attended = lax.psum_scatter(
        stacked.reshape(row_count * lax.axis_size("events"), local_width),
        "events",
        scatter_dimension=0,
        tiled=True,
    )
    first_moment = jnp.sum(attended, axis=1)
    second_moment = jnp.sum(attended * attended, axis=1)
    total_first, total_second = lax.psum((first_moment, second_moment), "heads")
    average = total_first / HD
    variance = total_second / HD - average * average
    normed = (attended - average[:, None]) * lax.rsqrt(variance + epsilon)[:, None] * gain
    gated = (normed * gate_values.astype(jnp.float32)).astype(jnp.bfloat16)
    projected = jnp.dot(gated, w_out, preferred_element_type=jnp.float32)
    summed_heads = lax.psum(projected, "heads")
    return (inputs.astype(jnp.float32) + summed_heads).astype(jnp.bfloat16)


def solution(mesh):
    placed = (
        P(("groups", "events"), None),
        P("groups"),
        P(("groups", "events")),
        P(("groups", "events")),
        P(None, None, "heads"),
        P(("groups", "events"), "heads"),
        P(("groups", "events"), "heads"),
        P("heads"),
        P("heads", None),
    )
    return jax.shard_map(
        shards, mesh=mesh, in_specs=placed, out_specs=P(("groups", "events"), None), check_vma=False
    )
```

profile of v0, /device:TPU:0, one launch (start us, length us, event | category | flops | bytes accessed | tf_op | source)
XLA Modules:
  0.0 143.9 jit_solution(11439747766623471906)
XLA Ops:
  6.5 0.0 copy-start
  6.5 0.0 reduce-scatter.2.cloned.1.call-start
  7.3 32.8 %all_gather.3 = bf16[128,1024]{1,0:T(8,128)(2,1)S(1)} all-gather(bf16[16,1024]{1,0:T(8,128)(2,1)} %param.9), channel_id=1, replica_groups=mesh['groups'=2,'events'=8,'heads'=2] {'events'}, dimensions={0}, use_global_device_ids=true | all-gather | bytes 294912 | tf_op jit(solution)/shard_map/all_gather | solution.py:25
  40.1 2.0 %copy.14 = bf16[512,512]{0,1:T(8,128)(2,1)} copy(bf16[512,512]{1,0:T(8,128)(2,1)} %param.15) | data formatting | bytes 1048576 | tf_op jit(solution)/shard_map/reshape | solution.py:32
  42.1 2.2 %copy.17 = bf16[128,8,2,512]{3,1,2,0:T(8,128)(2,1)S(1)} copy(bf16[128,8,2,512]{3,2,1,0:T(2,128)(2,1)} %bitcast.29) | data formatting | bytes 4194304
  44.3 0.0 copy-start.2
  44.3 0.0 copy-start.4
  44.3 1.0 fusion.14
  45.3 0.0 copy-done.2
  45.3 0.0 copy-done.4
  45.3 0.1 and_convert_fusion
  45.4 0.0 copy-start.1
  45.4 0.0 copy-start.3
  45.4 2.6 %fusion.4 = f32[4,128,128]{1,2,0:T(8,128)} fusion(bf16[512,4,128]{0,2,1:T(8,128)(2,1)} %bitcast.30, f32[128,512]{1,0:T(8,128)S(1)} %and_convert_fusion, bf16[16,4,8,128]{3,2,1,0:T(8,128)(2,1)} %fusion.14, bf16[512,512]{1,0:T(8,128)(2,1)} %param.14), kind=kOutput, calls=%fused_computation.6 | convolution fusion | flops 136052736 | bytes 1703936 | tf_op jit(solution)/shard_map/while/body/eval_jaxpr/hce,ehd->chd/dot_general | solution.py:45
  48.1 1.8 %copy.13 = f32[128,512]{1,0:T(8,128)} copy(f32[128,512]{0,1:T(8,128)} %bitcast.31) | data formatting | bytes 524288 | tf_op jit(solution)/shard_map/reshape | solution.py:61
  49.9 0.0 reduce-scatter.2.cloned.1.call-update
  49.9 0.0 all-reduce.3.cloned.1.call-start
  49.9 63.5 %reduce-scatter.2.cloned.1.call-done = f32[16,512]{1,0:T(8,128)} async-done(((f32[128,512]{1,0:T(8,128)}), f32[16,512]{1,0:T(8,128)}) %reduce-scatter.2.cloned.1.call-update) | async-done | bytes 32784 | tf_op jit(solution)/shard_map/reduce_scatter | solution.py:60
  113.5 0.9 fusion.38
  114.3 2.5 %all-reduce = (f32[16]{0:T(128)S(1)}, f32[16]{0:T(128)S(1)}) all-reduce(f32[16]{0:T(128)S(1)} %get-tuple-element.20, f32[16]{0:T(128)S(1)} %get-tuple-element.19), channel_id=1, replica_groups=mesh['groups'=2,'events'=8,'heads'=2] {'heads'}, use_global_device_ids=true, to_apply=%region_4.5 | all-reduce | flops 32 | bytes 256 | tf_op jit(solution)/shard_map/psum | solution.py:68
  116.8 0.0 copy-done
  116.8 0.0 copy-done.1
  116.8 0.0 copy-done.3
  116.8 1.9 %fusion.26 = f32[16,1024]{1,0:T(8,128)} fusion(bf16[512,1024]{1,0:T(8,128)(2,1)S(1)} %copy-done, bf16[16,1024]{1,0:T(8,128)(2,1)S(1)} %copy-done.1, bf16[1024,1024]{1,0:T(8,128)(2,1)S(1)} %bitcast.28, f32[16,512]{1,0:T(8,128)} %reduce-scatter.2.cloned.1.call-done, f32[512]{0:T(512)S(1)} %copy-done.3, f32[16]{0:T(128)S(1)} %get-tuple-element.32, ...), kind=kOutput, calls=%fused_computation.20 | convolution fusion | flops 33644544 | bytes 2231296 | tf_op jit(solution)/shard_map/dot_general | solution.py:73
  118.7 0.0 all-reduce.3.cloned.1.call-update
  118.7 16.9 %all-reduce.3.cloned.1.call-done = f32[16,1024]{1,0:T(8,128)} async-done(((f32[16,1024]{1,0:T(8,128)}), f32[16,1024]{1,0:T(8,128)}) %all-reduce.3.cloned.1.call-update) | async-done | bytes 65552 | tf_op jit(solution)/shard_map/psum | solution.py:74
  135.6 1.5 %add_convert_fusion = bf16[16,1024]{1,0:T(8,128)(2,1)} fusion(f32[16,1024]{1,0:T(8,128)} %all-reduce.3.cloned.1.call-done, bf16[16,1024]{1,0:T(8,128)(2,1)S(1)} %copy-done.1), kind=kLoop, calls=%fused_computation.17 | loop fusion | flops 49152 | bytes 131072 | tf_op jit(solution)/shard_map/convert_element_type | solution.py:75
  (2 shorter events, 0.0 us)
Async XLA Ops:
  6.5 110.3 %copy-start = (bf16[512,1024]{1,0:T(8,128)(2,1)S(1)}, bf16[512,1024]{1,0:T(8,128)(2,1)}, u32[]{:S(2)}) copy-start(bf16[512,1024]{1,0:T(8,128)(2,1)} %param.17) | copy-start | bytes 3145732
  6.5 106.9 %reduce-scatter.2.cloned.1.call-start = ((), (), s32[]{:S(2)}) async-start(), calls=%async_computation.1 | async-start | bytes 294912 | tf_op jit(solution)/shard_map/reduce_scatter | solution.py:60
  44.3 1.0 copy-start.2
  44.3 1.0 copy-start.4
  45.4 71.4 %copy-start.1 = (bf16[16,1024]{1,0:T(8,128)(2,1)S(1)}, bf16[16,1024]{1,0:T(8,128)(2,1)}, u32[]{:S(2)}) copy-start(bf16[16,1024]{1,0:T(8,128)(2,1)} %param.9) | copy-start | bytes 98308
  45.4 71.4 %copy-start.3 = (f32[512]{0:T(512)S(1)}, f32[512]{0:T(512)}, u32[]{:S(2)}) copy-start(f32[512]{0:T(512)} %param.16) | copy-start | bytes 6148
  49.9 85.7 %all-reduce.3.cloned.1.call-start = ((), (), s32[]{:S(2)}) async-start(), calls=%async_computation.2 | async-start | bytes 131072 | tf_op jit(solution)/shard_map/psum | solution.py:74
Sparse Core Ops, SparseCore 0:
  50.0 63.4 reduce-scatter.1
  118.8 16.7 all-reduce.2
where the time goes:
time: 144 us
  waiting for transfers between devices  80.5 us (56%)
  blocking collectives  35.2 us (24%)
  between operations  14.2 us (10%)
  local copies, waits for them, and re-layouts  6 us (4%)
  matrix products  5.52 us (4%)
  other arithmetic  2.45 us (2%)
    reduce_scatter x1, waiting for transfers between devices, shards(): lax.psum_scatter(stacked.reshape(row_count * lax.axis_size('events'), loc...  63.5 us
    all_gather x1, blocking collectives, shards(): gathered_rows = lax.all_gather(inputs, 'events', axis=0, tiled=True)  32.8 us
    psum x1, waiting for transfers between devices, shards(): summed_heads = lax.psum(projected, 'heads')  16.9 us
  transfers between devices with their start and end apart: 2, of which 2 were waited for; matrix products, arithmetic and copies ran while one was open for 0% of the time, Pallas kernels for 0%

commit v1 on v0

--- a/solution.py
+++ b/solution.py
@@ -22,7 +22,25 @@
     gate_values = jax.nn.silu(
         jnp.dot(inputs, gate_weight, preferred_element_type=jnp.float32)
     ).astype(jnp.bfloat16)
-    gathered_rows = lax.all_gather(inputs, "events", axis=0, tiled=True)
+    peers, mine, extent = (lax.axis_size("events"), lax.axis_index("events"), inputs.shape[0])
+    upward = [(i, (i + 1) % peers) for i in range(peers)]
+    left = [(i, (i - 1) % peers) for i in range(peers)]
+    gathered_rows = jnp.zeros(
+        (*inputs.shape[:0], peers * extent, *inputs.shape[0 + 1 :]), inputs.dtype
+    )
+    gathered_rows = lax.dynamic_update_slice_in_dim(gathered_rows, inputs, mine * extent, axis=0)
+    from_left = from_right = inputs
+    halfway = peers // 2
+    for step in range(1, halfway + 1):
+        from_left = lax.ppermute(from_left, "events", upward)
+        gathered_rows = lax.dynamic_update_slice_in_dim(
+            gathered_rows, from_left, (mine - step) % peers * extent, axis=0
+        )
+        if step < peers - halfway:
+            from_right = lax.ppermute(from_right, "events", left)
+            gathered_rows = lax.dynamic_update_slice_in_dim(
+                gathered_rows, from_right, (mine + step) % peers * extent, axis=0
+            )
     queries = jax.nn.silu(
         jnp.dot(gathered_rows, query_weight, preferred_element_type=jnp.float32)
     ).astype(jnp.bfloat16)

time: 144 us -> 138 us (0.958)
  blocking collectives: 35.2 us -> 2.46 us
  starting transfers between devices: 0.04 us -> 15.5 us
  local copies, waits for them, and re-layouts: 6 us -> 12.4 us
  waiting for transfers between devices: 80.5 us -> 83.3 us
    all_gather x1 -> x0, blocking collectives: 32.8 us -> none  [shards(): gathered_rows = lax.all_gather(inputs, 'events', axis=0, tiled=True)]
    ppermute x0 -> x7, starting transfers between devices: none -> 15.5 us  [the longest x3 12.5 us: shards(): from_right = lax.ppermute(from_right, 'events', left)]
    ppermute x0 -> x7, waiting for transfers between devices: none -> 6.72 us  [the longest x4 6.71 us: shards(): from_left = lax.ppermute(from_left, 'events', upward)]
    dynamic_update_slice x0 -> x8, local copies, waits for them, and re-layouts: none -> 5.65 us  [the longest x4 2.45 us: shards(): lax.dynamic_update_slice_in_dim(gathered_rows, from_left, (mine - step) %...]
    reduce_scatter x1, waiting for transfers between devices: 63.5 us -> 59.6 us  [shards(): lax.psum_scatter(stacked.reshape(row_count * lax.axis_size('events'), loc...]
  transfers between devices with their start and end apart: 2 -> 9, of which waited for: 2 -> 5; matrix products, arithmetic and copies ran while one was open for 0% -> 8% of each run, Pallas kernels for 0% -> 0%
where the time goes in v1:
time: 138 us; the launch traced here: 137 us
  waiting for transfers between devices  83.3 us (60%)
  starting transfers between devices  15.5 us (11%)
  between operations  14.2 us (10%)
  local copies, waits for them, and re-layouts  12.4 us (9%)
  matrix products  6.46 us (5%)
  other arithmetic  3.14 us (2%)
  blocking collectives  2.46 us (2%)
    reduce_scatter x1, waiting for transfers between devices, shards(): lax.psum_scatter(stacked.reshape(row_count * lax.axis_size('events'), loc...  59.6 us
    psum x1, waiting for transfers between devices, shards(): summed_heads = lax.psum(projected, 'heads')  16.9 us
    ppermute x3, starting transfers between devices, shards(): from_right = lax.ppermute(from_right, 'events', left)  12.5 us
    ppermute x4, waiting for transfers between devices, shards(): from_left = lax.ppermute(from_left, 'events', upward)  6.71 us
    ppermute x4, starting transfers between devices, shards(): from_left = lax.ppermute(from_left, 'events', upward)  3.03 us
  transfers between devices with their start and end apart: 9, of which 5 were waited for; matrix products, arithmetic and copies ran while one was open for 8% of the time, Pallas kernels for 0%

profile of v1, /device:TPU:0, one launch (start us, length us, event | category | flops | bytes accessed | tf_op | source)
XLA Modules:
  0.0 137.4 jit_solution(7435239161077311004)
XLA Ops:
  6.5 0.0 copy-start
  6.5 0.0 reduce-scatter.2.cloned.1.call-start
  6.5 3.0 %collective-permute-start = (bf16[16,1024]{1,0:T(8,128)(2,1)}, bf16[16,1024]{1,0:T(8,128)(2,1)S(1)}, u32[]{:S(2)}, u32[]{:S(2)}) collective-permute-start(bf16[16,1024]{1,0:T(8,128)(2,1)} %param.9), channel_id=1, source_target_pairs={{0,2},{2,4},{4,6},{6,8},{8,10},{10,12},{12,14},{14,0},{1,3},{3,5},... | collective-permute-start | bytes 98312 | tf_op jit(solution)/shard_map/ppermute | solution.py:35
  9.5 3.0 %collective-permute-start.1 = (bf16[16,1024]{1,0:T(8,128)(2,1)}, bf16[16,1024]{1,0:T(8,128)(2,1)S(1)}, u32[]{:S(2)}, u32[]{:S(2)}) collective-permute-start(bf16[16,1024]{1,0:T(8,128)(2,1)} %param.9), channel_id=1, source_target_pairs={{0,14},{2,0},{4,2},{6,4},{8,6},{10,8},{12,10},{14,12},{1,15},{3,1}... | collective-permute-start | bytes 98312 | tf_op jit(solution)/shard_map/ppermute | solution.py:40
  13.2 0.8 and_convert_fusion
  14.0 0.7 broadcast_in_dim.13
  14.7 1.4 %constant_dynamic-update-slice_fusion.7 = bf16[128,1024]{1,0:T(8,128)(2,1)} fusion(bf16[128,1024]{1,0:T(8,128)(2,1)} %broadcast_in_dim.13, bf16[16,1024]{1,0:T(8,128)(2,1)} %param.9, s32[]{:T(128)S(6)} %select_n.58), kind=kLoop, calls=%fused_computation.37 | loop fusion | bytes 65540 | tf_op jit(solution)/shard_map/dynamic_update_slice | solution.py:31
  16.1 2.1 %copy.14 = bf16[512,512]{0,1:T(8,128)(2,1)} copy(bf16[512,512]{1,0:T(8,128)(2,1)} %param.15) | data formatting | bytes 1048576 | tf_op jit(solution)/shard_map/reshape | solution.py:50
  18.2 2.1 %copy.17 = bf16[128,8,2,512]{3,1,2,0:T(8,128)(2,1)S(1)} copy(bf16[128,8,2,512]{3,2,1,0:T(2,128)(2,1)} %bitcast.29) | data formatting | bytes 4194304
  20.4 0.0 collective-permute-done
  20.4 0.1 collective-permute-start.2
  20.4 0.0 collective-permute-done.1
  20.4 4.7 %collective-permute-start.3 = (bf16[16,1024]{1,0:T(8,128)(2,1)S(1)}, bf16[16,1024]{1,0:T(8,128)(2,1)S(1)}, u32[]{:S(2)}, u32[]{:S(2)}) collective-permute-start(bf16[16,1024]{1,0:T(8,128)(2,1)S(1)} %collective-permute-done.1), channel_id=1, source_target_pairs={{0,14},{2,0},{4,2},{6,4},{8,6},{10,8},{12,10},{14,12},{1,15},{3,1}... | collective-permute-start | bytes 98312 | tf_op jit(solution)/shard_map/ppermute | solution.py:40
  25.1 0.6 constant_dynamic-update-slice_fusion.6
  25.8 0.6 constant_dynamic-update-slice_fusion.5
  26.4 0.7 collective-permute-done.2
  27.0 0.0 collective-permute-start.4
  27.0 0.0 collective-permute-done.3
  27.0 4.7 %collective-permute-start.5 = (bf16[16,1024]{1,0:T(8,128)(2,1)S(1)}, bf16[16,1024]{1,0:T(8,128)(2,1)S(1)}, u32[]{:S(2)}, u32[]{:S(2)}) collective-permute-start(bf16[16,1024]{1,0:T(8,128)(2,1)S(1)} %collective-permute-done.3), channel_id=1, source_target_pairs={{0,14},{2,0},{4,2},{6,4},{8,6},{10,8},{12,10},{14,12},{1,15},{3,1}... | collective-permute-start | bytes 98312 | tf_op jit(solution)/shard_map/ppermute | solution.py:40
  31.8 0.6 constant_dynamic-update-slice_fusion.4
  32.4 0.6 constant_dynamic-update-slice_fusion.3
  33.0 0.7 collective-permute-done.4
  33.6 0.0 collective-permute-start.6
  33.6 0.6 constant_dynamic-update-slice_fusion.2
  34.3 0.0 collective-permute-done.5
  34.3 0.6 constant_dynamic-update-slice_fusion.1
  34.9 5.4 %collective-permute-done.6 = bf16[16,1024]{1,0:T(8,128)(2,1)S(1)} collective-permute-done((bf16[16,1024]{1,0:T(8,128)(2,1)S(1)}, bf16[16,1024]{1,0:T(8,128)(2,1)S(1)}, u32[]{:S(2)}, u32[]{:S(2)}) %collective-permute-start.6) | collective-permute-done | bytes 32800 | tf_op jit(solution)/shard_map/ppermute | solution.py:35
  40.3 0.6 constant_dynamic-update-slice_fusion
  40.9 2.0 %fusion.14 = bf16[16,4,8,128]{3,2,1,0:T(8,128)(2,1)} fusion(bf16[128,1024]{1,0:T(8,128)(2,1)} %constant_dynamic-update-slice_fusion, bf16[1024,1024]{1,0:T(8,128)(2,1)S(1)} %bitcast.27), kind=kOutput, calls=%fused_computation.13 | convolution fusion | flops 134545408 | bytes 1441792 | tf_op jit(solution)/shard_map/dot_general | solution.py:45
  42.8 0.0 copy-start.1
  42.8 0.0 copy-start.2
  42.8 2.6 %fusion.4 = f32[4,128,128]{1,2,0:T(8,128)} fusion(bf16[512,4,128]{0,2,1:T(8,128)(2,1)} %bitcast.30, f32[128,512]{1,0:T(8,128)S(1)} %and_convert_fusion, bf16[16,4,8,128]{3,2,1,0:T(8,128)(2,1)} %fusion.14, bf16[512,512]{1,0:T(8,128)(2,1)} %param.14), kind=kOutput, calls=%fused_computation.6 | convolution fusion | flops 136052736 | bytes 1703936 | tf_op jit(solution)/shard_map/while/body/eval_jaxpr/hce,ehd->chd/dot_general | solution.py:63
  45.5 1.8 %copy.13 = f32[128,512]{1,0:T(8,128)} copy(f32[128,512]{0,1:T(8,128)} %bitcast.31) | data formatting | bytes 524288 | tf_op jit(solution)/shard_map/reshape | solution.py:79
  47.2 0.0 reduce-scatter.2.cloned.1.call-update
  47.3 0.0 all-reduce.3.cloned.1.call-start
  47.3 59.6 %reduce-scatter.2.cloned.1.call-done = f32[16,512]{1,0:T(8,128)} async-done(((f32[128,512]{1,0:T(8,128)}), f32[16,512]{1,0:T(8,128)}) %reduce-scatter.2.cloned.1.call-update) | async-done | bytes 32784 | tf_op jit(solution)/shard_map/reduce_scatter | solution.py:78
  107.0 0.9 fusion.38
  107.8 2.5 %all-reduce = (f32[16]{0:T(128)S(1)}, f32[16]{0:T(128)S(1)}) all-reduce(f32[16]{0:T(128)S(1)} %get-tuple-element.20, f32[16]{0:T(128)S(1)} %get-tuple-element.19), channel_id=1, replica_groups=mesh['groups'=2,'events'=8,'heads'=2] {'heads'}, use_global_device_ids=true, to_apply=%region_4.5 | all-reduce | flops 32 | bytes 256 | tf_op jit(solution)/shard_map/psum | solution.py:86
  110.3 0.0 copy-done
  110.3 0.0 copy-done.1
  110.3 0.0 copy-done.2
  110.3 1.9 %fusion.26 = f32[16,1024]{1,0:T(8,128)} fusion(bf16[512,1024]{1,0:T(8,128)(2,1)S(1)} %copy-done, bf16[16,1024]{1,0:T(8,128)(2,1)S(1)} %copy-done.1, bf16[1024,1024]{1,0:T(8,128)(2,1)S(1)} %bitcast.28, f32[16,512]{1,0:T(8,128)} %reduce-scatter.2.cloned.1.call-done, f32[512]{0:T(512)S(1)} %copy-done.2, f32[16]{0:T(128)S(1)} %get-tuple-element.32, ...), kind=kOutput, calls=%fused_computation.20 | convolution fusion | flops 33644544 | bytes 2231296 | tf_op jit(solution)/shard_map/dot_general | solution.py:91
  112.2 0.0 all-reduce.3.cloned.1.call-update
  112.2 16.9 %all-reduce.3.cloned.1.call-done = f32[16,1024]{1,0:T(8,128)} async-done(((f32[16,1024]{1,0:T(8,128)}), f32[16,1024]{1,0:T(8,128)}) %all-reduce.3.cloned.1.call-update) | async-done | bytes 65552 | tf_op jit(solution)/shard_map/psum | solution.py:92
  129.1 1.5 %add_convert_fusion = bf16[16,1024]{1,0:T(8,128)(2,1)} fusion(f32[16,1024]{1,0:T(8,128)} %all-reduce.3.cloned.1.call-done, bf16[16,1024]{1,0:T(8,128)(2,1)S(1)} %copy-done.1), kind=kLoop, calls=%fused_computation.17 | loop fusion | flops 49152 | bytes 131072 | tf_op jit(solution)/shard_map/convert_element_type | solution.py:93
  (2 shorter events, 0.0 us)
Async XLA Ops:
  6.5 103.8 %copy-start = (bf16[512,1024]{1,0:T(8,128)(2,1)S(1)}, bf16[512,1024]{1,0:T(8,128)(2,1)}, u32[]{:S(2)}) copy-start(bf16[512,1024]{1,0:T(8,128)(2,1)} %param.17) | copy-start | bytes 3145732
  6.5 100.4 %reduce-scatter.2.cloned.1.call-start = ((), (), s32[]{:S(2)}) async-start(), calls=%async_computation.1 | async-start | bytes 294912 | tf_op jit(solution)/shard_map/reduce_scatter | solution.py:78
  6.5 13.8 %collective-permute-start = (bf16[16,1024]{1,0:T(8,128)(2,1)}, bf16[16,1024]{1,0:T(8,128)(2,1)S(1)}, u32[]{:S(2)}, u32[]{:S(2)}) collective-permute-start(bf16[16,1024]{1,0:T(8,128)(2,1)} %param.9), channel_id=1, source_target_pairs={{0,2},{2,4},{4,6},{6,8},{8,10},{10,12},{12,14},{14,0},{1,3},{3,5},... | collective-permute-start | bytes 98312 | tf_op jit(solution)/shard_map/ppermute | solution.py:35
  9.5 10.9 %collective-permute-start.1 = (bf16[16,1024]{1,0:T(8,128)(2,1)}, bf16[16,1024]{1,0:T(8,128)(2,1)S(1)}, u32[]{:S(2)}, u32[]{:S(2)}) collective-permute-start(bf16[16,1024]{1,0:T(8,128)(2,1)} %param.9), channel_id=1, source_target_pairs={{0,14},{2,0},{4,2},{6,4},{8,6},{10,8},{12,10},{14,12},{1,15},{3,1}... | collective-permute-start | bytes 98312 | tf_op jit(solution)/shard_map/ppermute | solution.py:40
  20.4 6.7 %collective-permute-start.2 = (bf16[16,1024]{1,0:T(8,128)(2,1)S(1)}, bf16[16,1024]{1,0:T(8,128)(2,1)S(1)}, u32[]{:S(2)}, u32[]{:S(2)}) collective-permute-start(bf16[16,1024]{1,0:T(8,128)(2,1)S(1)} %collective-permute-done), channel_id=1, source_target_pairs={{0,2},{2,4},{4,6},{6,8},{8,10},{10,12},{12,14},{14,0},{1,3},{3,5},... | collective-permute-start | bytes 98312 | tf_op jit(solution)/shard_map/ppermute | solution.py:35
  20.4 6.6 %collective-permute-start.3 = (bf16[16,1024]{1,0:T(8,128)(2,1)S(1)}, bf16[16,1024]{1,0:T(8,128)(2,1)S(1)}, u32[]{:S(2)}, u32[]{:S(2)}) collective-permute-start(bf16[16,1024]{1,0:T(8,128)(2,1)S(1)} %collective-permute-done.1), channel_id=1, source_target_pairs={{0,14},{2,0},{4,2},{6,4},{8,6},{10,8},{12,10},{14,12},{1,15},{3,1}... | collective-permute-start | bytes 98312 | tf_op jit(solution)/shard_map/ppermute | solution.py:40
  27.0 6.6 %collective-permute-start.4 = (bf16[16,1024]{1,0:T(8,128)(2,1)S(1)}, bf16[16,1024]{1,0:T(8,128)(2,1)S(1)}, u32[]{:S(2)}, u32[]{:S(2)}) collective-permute-start(bf16[16,1024]{1,0:T(8,128)(2,1)S(1)} %collective-permute-done.2), channel_id=1, source_target_pairs={{0,2},{2,4},{4,6},{6,8},{8,10},{10,12},{12,14},{14,0},{1,3},{3,5},... | collective-permute-start | bytes 98312 | tf_op jit(solution)/shard_map/ppermute | solution.py:35
  27.0 7.2 %collective-permute-start.5 = (bf16[16,1024]{1,0:T(8,128)(2,1)S(1)}, bf16[16,1024]{1,0:T(8,128)(2,1)S(1)}, u32[]{:S(2)}, u32[]{:S(2)}) collective-permute-start(bf16[16,1024]{1,0:T(8,128)(2,1)S(1)} %collective-permute-done.3), channel_id=1, source_target_pairs={{0,14},{2,0},{4,2},{6,4},{8,6},{10,8},{12,10},{14,12},{1,15},{3,1}... | collective-permute-start | bytes 98312 | tf_op jit(solution)/shard_map/ppermute | solution.py:40
  33.6 6.6 %collective-permute-start.6 = (bf16[16,1024]{1,0:T(8,128)(2,1)S(1)}, bf16[16,1024]{1,0:T(8,128)(2,1)S(1)}, u32[]{:S(2)}, u32[]{:S(2)}) collective-permute-start(bf16[16,1024]{1,0:T(8,128)(2,1)S(1)} %collective-permute-done.4), channel_id=1, source_target_pairs={{0,2},{2,4},{4,6},{6,8},{8,10},{10,12},{12,14},{14,0},{1,3},{3,5},... | collective-permute-start | bytes 98312 | tf_op jit(solution)/shard_map/ppermute | solution.py:35
  42.8 67.5 %copy-start.1 = (bf16[16,1024]{1,0:T(8,128)(2,1)S(1)}, bf16[16,1024]{1,0:T(8,128)(2,1)}, u32[]{:S(2)}) copy-start(bf16[16,1024]{1,0:T(8,128)(2,1)} %param.9) | copy-start | bytes 98308
  42.8 67.5 %copy-start.2 = (f32[512]{0:T(512)S(1)}, f32[512]{0:T(512)}, u32[]{:S(2)}) copy-start(f32[512]{0:T(512)} %param.16) | copy-start | bytes 6148
  47.3 81.9 %all-reduce.3.cloned.1.call-start = ((), (), s32[]{:S(2)}) async-start(), calls=%async_computation.2 | async-start | bytes 131072 | tf_op jit(solution)/shard_map/psum | solution.py:92
Sparse Core Ops, SparseCore 0:
  47.4 59.5 reduce-scatter.1
  112.3 16.7 all-reduce.2
